TPU v7x, 128 devices: a whole 4x4x4 slice. The times are simulated.
128 devices in a mesh: dom: 16 (over z, y), grp: 8 (over x, core).
Axes of the slice: x: 4, y: 4, z: 4, core: 2. Of those that a mesh axis runs over, the one named last changes fastest.
Arguments:
- residual_in: bfloat16 [1024, 32, 625], P(('dom', 'grp')), may hold values from -6 to 6
- block_inverse: bfloat16 [1024, 625, 625], P(('dom', 'grp')), may hold values from -0.25 to 0.25
- coupling: bfloat16 [2048, 625, 625], P(('dom', 'grp')), may hold values from -0.25 to 0.25
- tile_region: int32 [2048, 1], P(('dom', 'grp')), may hold values from 0 to 15; in each aligned block of 16 rows (0 to 15, 16 to 31, ...) at most 2 rows name the same one
- tile_source: int32 [2048], P(('dom', 'grp')), may hold values from 0 to 7
- tile_target: int32 [2048], P(('dom', 'grp')), may hold values from 0 to 7
- interface_basis: bfloat16 [1024, 625, 64], P(('dom', 'grp')), may hold values from -0.25 to 0.25
- reduced_inverse: float32 [16, 64, 64], P('dom'), may hold values from -0.75 to 0.75
Outputs:
- preconditioned: float32 [1024, 32, 625], P(('dom', 'grp'))
Inputs may be any that keep to these rules, and one draw needn't show every extreme that they name: `tile_region`: among the 16 tiles of one device, at most 2 name the same region; in every draw some device names some region exactly 2 times.
All inputs are finite; a program needn't handle non-finite values.
Results may differ from a plain program's by a relative error of at most 0.013.
Values may be sent and summed in bfloat16 or wider, within the bound.
No kernel may reach another device: no remote copies, remote signals or barrier semaphores. Data moves between devices by JAX's collectives and lax.ppermute only.
A program may use at most 256 MiB of HBM per device.

v0:
```python
import jax
import jax.numpy as jnp
from jax import lax
from jax.sharding import PartitionSpec as P

CAP = 2


def shards(
    residual_in,
    block_inverse,
    coupling,
    tile_region,
    tile_source,
    tile_target,
    interface_basis,
    reduced_inverse,
):
    regions = lax.axis_size("dom")
    slots = regions * CAP
    elements = residual_in.shape[0]
    vectors = residual_in.shape[1]
    width = residual_in.shape[2]
    initial = jnp.einsum(
        "ekb,ebc->ekc", residual_in, block_inverse, preferred_element_type=jnp.float32
    ).astype(jnp.bfloat16)
    destination = tile_region[:, 0]
    onehot = (destination[:, None] == jnp.arange(regions, dtype=jnp.int32)[None, :]).astype(
        jnp.int32
    )
    earlier = jnp.cumsum(onehot, axis=0) - onehot
    tile_rank = jnp.sum(earlier * onehot, axis=1)
    slot_index = destination * CAP + tile_rank
    target_buffer = (
        jnp.full((slots,), -1, jnp.int32).at[slot_index].set(tile_target).reshape(regions, CAP)
    )
    targets = lax.all_to_all(target_buffer, "dom", split_axis=0, concat_axis=0, tiled=True).reshape(
        slots
    )
    sources = initial[tile_source]
    local_products = jnp.einsum(
        "tkb,tbc->tkc", sources, coupling, preferred_element_type=jnp.float32
    )
    product_buffer = (
        jnp.zeros((slots, vectors, width), jnp.float32).at[slot_index].set(local_products)
    )
    products = (
        lax.all_to_all(
            product_buffer.reshape(regions, CAP, vectors, width).astype(jnp.bfloat16),
            "dom",
            split_axis=0,
            concat_axis=0,
            tiled=True,
        )
        .astype(jnp.float32)
        .reshape(slots, vectors, width)
    )
    selector = (targets[None, :] == jnp.arange(elements, dtype=jnp.int32)[:, None]).astype(
        jnp.float32
    )
    coupled = jnp.dot(
        selector,
        products.reshape(slots, vectors * width),
        precision=lax.Precision.HIGHEST,
        preferred_element_type=jnp.float32,
    ).reshape(elements, vectors, width)
    corrected_in = (residual_in.astype(jnp.float32) - coupled).astype(jnp.bfloat16)
    second = jnp.einsum(
        "ekb,ebc->ekc", corrected_in, block_inverse, preferred_element_type=jnp.float32
    )
    second_b = second.astype(jnp.bfloat16)
    partial_reduced = jnp.einsum(
        "ekb,ebm->km", second_b, interface_basis, preferred_element_type=jnp.float32
    )
    reduced = lax.psum(partial_reduced, "grp")
    solved = jnp.dot(
        reduced,
        reduced_inverse[0],
        precision=lax.Precision.HIGHEST,
        preferred_element_type=jnp.float32,
    ).astype(jnp.bfloat16)
    correction = jnp.einsum(
        "km,ebm->ekb", solved, interface_basis, preferred_element_type=jnp.float32
    )
    return second + correction


def solution(mesh):
    return jax.shard_map(
        shards,
        mesh=mesh,
        in_specs=(
            P(("dom", "grp"), None, None),
            P(("dom", "grp"), None, None),
            P(("dom", "grp"), None, None),
            P(("dom", "grp"), None),
            P(("dom", "grp")),
            P(("dom", "grp")),
            P(("dom", "grp"), None, None),
            P("dom", None, None),
        ),
        out_specs=P(("dom", "grp"), None, None),
        check_vma=False,
    )
```

profile of v0, /device:TPU:0, one launch (start us, length us, event | category | flops | bytes accessed | tf_op | source)
XLA Modules:
  0.0 96.3 jit_solution(15889635007566257269)
XLA Ops:
  0.0 0.0 copy-start
  0.0 0.8 fusion.22
  0.8 0.8 select_reduce_fusion
  1.7 0.7 fusion.26
  2.3 0.8 scatter_custom_fusion
  3.1 0.7 all_to_all.9
  3.8 8.2 %all-to-all-start = ((s32[16,1,2]{2,1,0:T(1,128)}), s32[16,1,2]{2,1,0:T(1,128)S(1)}, u32[]{:S(2)}, u32[]{:S(2)}) async-start(s32[16,1,2]{2,1,0:T(1,128)} %bitcast.3), calls=%async_computation | async-start | bytes 16384 | tf_op jit(solution)/shard_map/all_to_all | solution.py:37
  11.9 0.7 compare_select_fusion
  12.6 5.2 %fusion.15 = bf16[8,32,625]{2,1,0:T(8,128)(2,1)S(1)} fusion(bf16[8,32,625]{2,1,0:T(8,128)(2,1)} %param.8, bf16[8,625,625]{2,0,1:T(8,128)(2,1)} %param.9), kind=kOutput, calls=%fused_computation.15 | convolution fusion | flops 200160000 | bytes 6890000 | tf_op jit(solution)/shard_map/ekb,ebc->ekc/dot_general | solution.py:24
  17.8 0.7 gather_fusion
  18.5 10.1 %fusion = f32[16,32,625]{2,1,0:T(8,128)} fusion(bf16[16,32,625]{2,1,0:T(8,128)(2,1)S(1)} %gather_fusion, bf16[16,625,625]{2,0,1:T(8,128)(2,1)} %param.10), kind=kOutput, calls=%fused_computation.3 | convolution fusion | flops 400000000 | bytes 14420000 | tf_op jit(solution)/shard_map/tkb,tbc->tkc/dot_general | solution.py:41
  28.6 0.3 broadcast_in_dim.14
  28.9 2.4 %scatter_fusion = f32[32,32,625]{2,1,0:T(8,128)S(1)} fusion(f32[32,32,625]{2,1,0:T(8,128)S(1)} %broadcast_in_dim.14, s32[16]{0:T(128)S(1)} %fusion.26, f32[16,32,625]{2,1,0:T(8,128)} %fusion), kind=kCustom, calls=%fused_computation.2 | custom fusion | bytes 3840064 | tf_op jit(solution)/shard_map/scatter | solution.py:45
  31.3 1.2 %convert_element_type.29 = bf16[32,32,625]{2,1,0:T(8,128)(2,1)} convert(f32[32,32,625]{2,1,0:T(8,128)S(1)} %scatter_fusion) | non-fusion elementwise | flops 640000 | bytes 3840000 | tf_op jit(solution)/shard_map/convert_element_type | solution.py:49
  32.5 0.0 all-to-all-done
  32.5 7.2 %all-to-all-start.1 = ((bf16[16,2,32,625]{3,2,1,0:T(8,128)(2,1)}), bf16[16,2,32,625]{3,2,1,0:T(8,128)(2,1)S(1)}, u32[]{:S(2)}, u32[]{:S(2)}) async-start(bf16[16,2,32,625]{3,2,1,0:T(8,128)(2,1)} %bitcast.34), calls=%async_computation.1 | async-start | bytes 2621440 | tf_op jit(solution)/shard_map/all_to_all | solution.py:48
  39.7 0.5 broadcast.39
  40.3 0.7 reduce.3
  40.9 0.1 eq.34
  41.0 18.9 %all-to-all-done.1 = bf16[16,2,32,625]{3,2,1,0:T(8,128)(2,1)S(1)} async-done(((bf16[16,2,32,625]{3,2,1,0:T(8,128)(2,1)}), bf16[16,2,32,625]{3,2,1,0:T(8,128)(2,1)S(1)}, u32[]{:S(2)}, u32[]{:S(2)}) %all-to-all-start.1) | async-done | bytes 1280032 | tf_op jit(solution)/shard_map/all_to_all | solution.py:48
  59.9 1.5 %reshape_reshape.3 = bf16[32,20000]{1,0:T(8,128)(2,1)S(1)} reshape(bf16[16,2,32,625]{3,2,1,0:T(8,128)(2,1)S(1)} %all-to-all-done.1) | data formatting | bytes 2560000 | tf_op jit(solution)/shard_map/reshape;reshape | solution.py:63
  61.4 3.2 %dot_general.28 = bf16[32,625,32]{1,0,2:T(8,128)(2,1)S(1)} reshape(bf16[20000,32]{0,1:T(8,128)(2,1)S(1)} %bitcast.35) | data formatting | bytes 2560000 | tf_op jit(solution)/shard_map/dot_general | solution.py:61
  64.6 1.5 %fusion.12 = bf16[8,32,625]{2,0,1:T(8,128)(2,1)S(1)} fusion(bf16[32,625,32]{1,0,2:T(8,128)(2,1)S(1)} %dot_general.28, bf16[8,32,625]{2,1,0:T(8,128)(2,1)} %param.8, s32[32]{0:T(128)S(1)} %eq.34), kind=kOutput, calls=%fused_computation.14 | convolution fusion | flops 10720256 | bytes 1920128 | tf_op jit(solution)/shard_map/dot_general | solution.py:61
  66.1 0.0 copy-start.1
  66.1 5.1 %fusion.2 = f32[8,32,625]{2,1,0:T(8,128)S(1)} fusion(bf16[8,625,625]{2,0,1:T(8,128)(2,1)} %param.9, bf16[8,32,625]{2,0,1:T(8,128)(2,1)S(1)} %fusion.12), kind=kOutput, calls=%fused_computation.5 | convolution fusion | flops 200000000 | bytes 7210000 | tf_op jit(solution)/shard_map/ekb,ebc->ekc/dot_general | solution.py:68
  71.2 0.0 copy-done
  71.2 0.3 convolution_bitcast_fusion.1
  71.5 23.6 %psum.7 = f32[32,64]{1,0:T(8,128)S(1)} all-reduce(f32[32,64]{1,0:T(8,128)S(1)} %convolution_bitcast_fusion.1), channel_id=1, replica_groups=mesh['dom'=16,'grp'=8] {'grp'}, use_global_device_ids=true, to_apply=%region_4.5 | all-reduce | flops 2048 | bytes 16384 | tf_op jit(solution)/shard_map/psum | solution.py:75
  95.1 0.0 copy-done.1
  95.1 0.1 fusion.18
  95.2 1.1 %fusion.11 = f32[8,32,625]{2,1,0:T(8,128)} fusion(f32[8,32,625]{2,1,0:T(8,128)S(1)} %fusion.2, bf16[32,64,1]{1,0,2:T(8,128)(2,1)S(1)} %fusion.18, bf16[8,625,64]{1,2,0:T(8,128)(2,1)S(1)} %copy-done), kind=kOutput, calls=%fused_computation.13 | convolution fusion | flops 20640000 | bytes 1924096 | tf_op jit(solution)/shard_map/km,ebm->ekb/dot_general | solution.py:82
  (2 shorter events, 0.0 us)
Async XLA Ops:
  0.0 71.2 %copy-start = (bf16[8,625,64]{1,2,0:T(8,128)(2,1)S(1)}, bf16[8,625,64]{1,2,0:T(8,128)(2,1)}, u32[]{:S(2)}) copy-start(bf16[8,625,64]{1,2,0:T(8,128)(2,1)} %param.14) | copy-start | bytes 1920004
  3.8 28.7 %all-to-all-start = ((s32[16,1,2]{2,1,0:T(1,128)}), s32[16,1,2]{2,1,0:T(1,128)S(1)}, u32[]{:S(2)}, u32[]{:S(2)}) async-start(s32[16,1,2]{2,1,0:T(1,128)} %bitcast.3), calls=%async_computation | async-start | bytes 16384 | tf_op jit(solution)/shard_map/all_to_all | solution.py:37
  32.5 27.4 %all-to-all-start.1 = ((bf16[16,2,32,625]{3,2,1,0:T(8,128)(2,1)}), bf16[16,2,32,625]{3,2,1,0:T(8,128)(2,1)S(1)}, u32[]{:S(2)}, u32[]{:S(2)}) async-start(bf16[16,2,32,625]{3,2,1,0:T(8,128)(2,1)} %bitcast.34), calls=%async_computation.1 | async-start | bytes 2621440 | tf_op jit(solution)/shard_map/all_to_all | solution.py:48
  66.1 29.0 %copy-start.1 = (f32[1,64,64]{2,1,0:T(8,128)S(1)}, f32[1,64,64]{2,1,0:T(8,128)}, u32[]{:S(2)}) copy-start(f32[1,64,64]{2,1,0:T(8,128)} %param.15) | copy-start | bytes 49156
where the time goes:
time: 96.7 us; the launch traced here: 96.3 us
  blocking collectives  23.6 us (24%)
  matrix products  23.4 us (24%)
  waiting for transfers between devices  18.9 us (20%)
  starting transfers between devices  15.4 us (16%)
  local copies, waits for them, and re-layouts  10.1 us (10%)
  other arithmetic  4.89 us (5%)
    psum x1, blocking collectives, shards(): reduced = lax.psum(partial_reduced, 'grp')  23.6 us
    all_to_all x1, waiting for transfers between devices, shards(): lax.all_to_all(product_buffer.reshape(regions, CAP, vectors, width).astyp...  18.9 us
    dot_general x1, matrix products, shards(): jnp.einsum('tkb,tbc->tkc', sources, coupling, preferred_element_type=jnp....  10.1 us
    all_to_all x1, starting transfers between devices, shards(): lax.all_to_all(target_buffer, 'dom', split_axis=0, concat_axis=0, tiled=T...  8.16 us
    all_to_all x1, starting transfers between devices, shards(): lax.all_to_all(product_buffer.reshape(regions, CAP, vectors, width).astyp...  7.23 us
    dot_general x1, matrix products, shards(): jnp.einsum('ekb,ebc->ekc', residual_in, block_inverse, preferred_element_...  5.17 us
    dot_general x1, matrix products, shards(): jnp.einsum('ekb,ebc->ekc', corrected_in, block_inverse, preferred_element...  5.14 us
    dot_general x1, local copies, waits for them, and re-layouts, shards(): jnp.dot(selector, products.reshape(slots, vectors * width), precision=lax...  3.17 us
  transfers between devices with their start and end apart: 2, of which 1 were waited for; matrix products, arithmetic and copies ran while one was open for 23% of the time, Pallas kernels for 0%

commit v1 on v0

--- a/solution.py
+++ b/solution.py
@@ -72,7 +72,9 @@
     partial_reduced = jnp.einsum(
         "ekb,ebm->km", second_b, interface_basis, preferred_element_type=jnp.float32
     )
-    reduced = lax.psum(partial_reduced, "grp")
+    reduced = partial_reduced
+    for hop in (1, 2, 4):
+        reduced = reduced + lax.ppermute(reduced, "grp", [(dev, dev ^ hop) for dev in range(8)])
     solved = jnp.dot(
         reduced,
         reduced_inverse[0],

time: 96.7 us -> 83.4 us (0.86)
  blocking collectives: 23.6 us -> 0 us
  waiting for transfers between devices: 18.9 us -> 24.5 us
  starting transfers between devices: 15.4 us -> 19.9 us
    psum x1 -> x0, blocking collectives: 23.6 us -> none  [shards(): reduced = lax.psum(partial_reduced, 'grp')]
    ppermute x0 -> x3, waiting for transfers between devices: none -> 5.65 us  [shards(): lax.ppermute(reduced, 'grp', [(dev, dev ^ hop) for dev in range(8)])]
    ppermute x0 -> x3, starting transfers between devices: none -> 4.52 us  [shards(): lax.ppermute(reduced, 'grp', [(dev, dev ^ hop) for dev in range(8)])]
  transfers between devices with their start and end apart: 2 -> 5, of which waited for: 1 -> 4; matrix products, arithmetic and copies ran while one was open for 23% -> 26% of each run, Pallas kernels for 0% -> 0%
where the time goes in v1:
time: 83.4 us; the launch traced here: 82.9 us
  waiting for transfers between devices  24.5 us (29%)
  matrix products  23.4 us (28%)
  starting transfers between devices  19.9 us (24%)
  local copies, waits for them, and re-layouts  10.1 us (12%)
  other arithmetic  4.89 us (6%)
    all_to_all x1, waiting for transfers between devices, shards(): lax.all_to_all(product_buffer.reshape(regions, CAP, vectors, width).astyp...  18.9 us
    dot_general x1, matrix products, shards(): jnp.einsum('tkb,tbc->tkc', sources, coupling, preferred_element_type=jnp....  10.1 us
    all_to_all x1, starting transfers between devices, shards(): lax.all_to_all(target_buffer, 'dom', split_axis=0, concat_axis=0, tiled=T...  8.16 us
    all_to_all x1, starting transfers between devices, shards(): lax.all_to_all(product_buffer.reshape(regions, CAP, vectors, width).astyp...  7.23 us
    ppermute x3, waiting for transfers between devices, shards(): lax.ppermute(reduced, 'grp', [(dev, dev ^ hop) for dev in range(8)])  5.65 us
    dot_general x1, matrix products, shards(): jnp.einsum('ekb,ebc->ekc', residual_in, block_inverse, preferred_element_...  5.17 us
    dot_general x1, matrix products, shards(): jnp.einsum('ekb,ebc->ekc', corrected_in, block_inverse, preferred_element...  5.14 us
    ppermute x3, starting transfers between devices, shards(): lax.ppermute(reduced, 'grp', [(dev, dev ^ hop) for dev in range(8)])  4.52 us
  transfers between devices with their start and end apart: 5, of which 4 were waited for; matrix products, arithmetic and copies ran while one was open for 26% of the time, Pallas kernels for 0%

profile of v1, /device:TPU:0, one launch (start us, length us, event | category | flops | bytes accessed | tf_op | source)
XLA Modules:
  0.0 82.9 jit_solution(16118975384032719782)
XLA Ops:
  0.0 0.0 copy-start
  0.0 0.8 fusion.23
  0.8 0.8 %select_reduce_fusion = s32[16]{0:T(128)S(1)} fusion(s32[16,16]{1,0:T(8,128)S(1)} %reduce_window_sum.11, s32[16]{0:T(128)} %bitcast.36), kind=kLoop, calls=%fused_computation.23 | loop fusion | flops 1264 | bytes 1152 | tf_op jit(solution)/shard_map/reduce_sum | solution.py:32
  1.7 0.7 fusion.27
  2.3 0.8 scatter_custom_fusion
  3.1 0.7 all_to_all.9
  3.8 8.2 %all-to-all-start = ((s32[16,1,2]{2,1,0:T(1,128)}), s32[16,1,2]{2,1,0:T(1,128)S(1)}, u32[]{:S(2)}, u32[]{:S(2)}) async-start(s32[16,1,2]{2,1,0:T(1,128)} %bitcast.3), calls=%async_computation | async-start | bytes 16384 | tf_op jit(solution)/shard_map/all_to_all | solution.py:37
  11.9 0.7 compare_select_fusion
  12.6 5.2 %fusion.15 = bf16[8,32,625]{2,1,0:T(8,128)(2,1)S(1)} fusion(bf16[8,32,625]{2,1,0:T(8,128)(2,1)} %param.8, bf16[8,625,625]{2,0,1:T(8,128)(2,1)} %param.9), kind=kOutput, calls=%fused_computation.15 | convolution fusion | flops 200160000 | bytes 6890000 | tf_op jit(solution)/shard_map/ekb,ebc->ekc/dot_general | solution.py:24
  17.8 0.7 gather_fusion
  18.5 10.1 %fusion = f32[16,32,625]{2,1,0:T(8,128)} fusion(bf16[16,32,625]{2,1,0:T(8,128)(2,1)S(1)} %gather_fusion, bf16[16,625,625]{2,0,1:T(8,128)(2,1)} %param.10), kind=kOutput, calls=%fused_computation.3 | convolution fusion | flops 400000000 | bytes 14420000 | tf_op jit(solution)/shard_map/tkb,tbc->tkc/dot_general | solution.py:41
  28.6 0.3 broadcast_in_dim.14
  28.9 2.4 %scatter_fusion = f32[32,32,625]{2,1,0:T(8,128)S(1)} fusion(f32[32,32,625]{2,1,0:T(8,128)S(1)} %broadcast_in_dim.14, s32[16]{0:T(128)S(1)} %fusion.27, f32[16,32,625]{2,1,0:T(8,128)} %fusion), kind=kCustom, calls=%fused_computation.2 | custom fusion | bytes 3840064 | tf_op jit(solution)/shard_map/scatter | solution.py:45
  31.3 1.2 %convert_element_type.29 = bf16[32,32,625]{2,1,0:T(8,128)(2,1)} convert(f32[32,32,625]{2,1,0:T(8,128)S(1)} %scatter_fusion) | non-fusion elementwise | flops 640000 | bytes 3840000 | tf_op jit(solution)/shard_map/convert_element_type | solution.py:49
  32.5 0.0 all-to-all-done
  32.5 7.2 %all-to-all-start.1 = ((bf16[16,2,32,625]{3,2,1,0:T(8,128)(2,1)}), bf16[16,2,32,625]{3,2,1,0:T(8,128)(2,1)S(1)}, u32[]{:S(2)}, u32[]{:S(2)}) async-start(bf16[16,2,32,625]{3,2,1,0:T(8,128)(2,1)} %bitcast.33), calls=%async_computation.1 | async-start | bytes 2621440 | tf_op jit(solution)/shard_map/all_to_all | solution.py:48
  39.7 0.5 broadcast.39
  40.3 0.7 reduce.3
  40.9 0.1 eq.34
  41.0 18.9 %all-to-all-done.1 = bf16[16,2,32,625]{3,2,1,0:T(8,128)(2,1)S(1)} async-done(((bf16[16,2,32,625]{3,2,1,0:T(8,128)(2,1)}), bf16[16,2,32,625]{3,2,1,0:T(8,128)(2,1)S(1)}, u32[]{:S(2)}, u32[]{:S(2)}) %all-to-all-start.1) | async-done | bytes 1280032 | tf_op jit(solution)/shard_map/all_to_all | solution.py:48
  59.9 1.5 %reshape_reshape.3 = bf16[32,20000]{1,0:T(8,128)(2,1)S(1)} reshape(bf16[16,2,32,625]{3,2,1,0:T(8,128)(2,1)S(1)} %all-to-all-done.1) | data formatting | bytes 2560000 | tf_op jit(solution)/shard_map/reshape;reshape | solution.py:63
  61.4 3.2 %dot_general.28 = bf16[32,625,32]{1,0,2:T(8,128)(2,1)S(1)} reshape(bf16[20000,32]{0,1:T(8,128)(2,1)S(1)} %bitcast.34) | data formatting | bytes 2560000 | tf_op jit(solution)/shard_map/dot_general | solution.py:61
  64.6 1.5 %fusion.12 = bf16[8,32,625]{2,0,1:T(8,128)(2,1)S(1)} fusion(bf16[32,625,32]{1,0,2:T(8,128)(2,1)S(1)} %dot_general.28, bf16[8,32,625]{2,1,0:T(8,128)(2,1)} %param.8, s32[32]{0:T(128)S(1)} %eq.34), kind=kOutput, calls=%fused_computation.14 | convolution fusion | flops 10720256 | bytes 1920128 | tf_op jit(solution)/shard_map/dot_general | solution.py:61
  66.1 0.0 copy-start.1
  66.1 5.1 %fusion.2 = f32[8,32,625]{2,1,0:T(8,128)S(1)} fusion(bf16[8,625,625]{2,0,1:T(8,128)(2,1)} %param.9, bf16[8,32,625]{2,0,1:T(8,128)(2,1)S(1)} %fusion.12), kind=kOutput, calls=%fused_computation.5 | convolution fusion | flops 200000000 | bytes 7210000 | tf_op jit(solution)/shard_map/ekb,ebc->ekc/dot_general | solution.py:68
  71.2 0.0 copy-done
  71.2 0.3 convolution_bitcast_fusion.1
  71.5 0.0 collective-permute-start
  71.5 1.2 %collective-permute-done = f32[32,64]{1,0:T(8,128)S(1)} collective-permute-done((f32[32,64]{1,0:T(8,128)S(1)}, f32[32,64]{1,0:T(8,128)S(1)}, u32[]{:S(2)}, u32[]{:S(2)}) %collective-permute-start) | collective-permute-done | bytes 8224 | tf_op jit(solution)/shard_map/ppermute | solution.py:77
  72.7 1.5 %collective-permute-start.1 = (f32[32,64]{1,0:T(8,128)S(1)}, f32[32,64]{1,0:T(8,128)S(1)}, u32[]{:S(2)}, u32[]{:S(2)}) collective-permute-start(f32[32,64]{1,0:T(8,128)S(1)} %add.27), channel_id=1, source_target_pairs={{0,2},{1,3},{2,0},{3,1},{4,6},{5,7},{6,4},{7,5},{8,10},{9,11},{10,... | collective-permute-start | bytes 24584 | tf_op jit(solution)/shard_map/ppermute | solution.py:77
  74.2 2.2 %collective-permute-done.1 = f32[32,64]{1,0:T(8,128)S(1)} collective-permute-done((f32[32,64]{1,0:T(8,128)S(1)}, f32[32,64]{1,0:T(8,128)S(1)}, u32[]{:S(2)}, u32[]{:S(2)}) %collective-permute-start.1) | collective-permute-done | bytes 8224 | tf_op jit(solution)/shard_map/ppermute | solution.py:77
  76.5 3.0 %collective-permute-start.2 = (f32[32,64]{1,0:T(8,128)S(1)}, f32[32,64]{1,0:T(8,128)S(1)}, u32[]{:S(2)}, u32[]{:S(2)}) collective-permute-start(f32[32,64]{1,0:T(8,128)S(1)} %add.28), channel_id=1, source_target_pairs={{0,4},{1,5},{2,6},{3,7},{4,0},{5,1},{6,2},{7,3},{8,12},{9,13},{10,... | collective-permute-start | bytes 24584 | tf_op jit(solution)/shard_map/ppermute | solution.py:77
  79.5 2.2 %collective-permute-done.2 = f32[32,64]{1,0:T(8,128)S(1)} collective-permute-done((f32[32,64]{1,0:T(8,128)S(1)}, f32[32,64]{1,0:T(8,128)S(1)}, u32[]{:S(2)}, u32[]{:S(2)}) %collective-permute-start.2) | collective-permute-done | bytes 8224 | tf_op jit(solution)/shard_map/ppermute | solution.py:77
  81.7 0.0 copy-done.1
  81.7 0.1 fusion.18
  81.9 1.1 %fusion.11 = f32[8,32,625]{2,1,0:T(8,128)} fusion(f32[8,32,625]{2,1,0:T(8,128)S(1)} %fusion.2, bf16[32,64,1]{1,0,2:T(8,128)(2,1)S(1)} %fusion.18, bf16[8,625,64]{1,2,0:T(8,128)(2,1)S(1)} %copy-done), kind=kOutput, calls=%fused_computation.13 | convolution fusion | flops 20640000 | bytes 1924096 | tf_op jit(solution)/shard_map/km,ebm->ekb/dot_general | solution.py:84
  (4 shorter events, 0.1 us)
Async XLA Ops:
  0.0 71.2 %copy-start = (bf16[8,625,64]{1,2,0:T(8,128)(2,1)S(1)}, bf16[8,625,64]{1,2,0:T(8,128)(2,1)}, u32[]{:S(2)}) copy-start(bf16[8,625,64]{1,2,0:T(8,128)(2,1)} %param.14) | copy-start | bytes 1920004
  3.8 28.7 %all-to-all-start = ((s32[16,1,2]{2,1,0:T(1,128)}), s32[16,1,2]{2,1,0:T(1,128)S(1)}, u32[]{:S(2)}, u32[]{:S(2)}) async-start(s32[16,1,2]{2,1,0:T(1,128)} %bitcast.3), calls=%async_computation | async-start | bytes 16384 | tf_op jit(solution)/shard_map/all_to_all | solution.py:37
  32.5 27.4 %all-to-all-start.1 = ((bf16[16,2,32,625]{3,2,1,0:T(8,128)(2,1)}), bf16[16,2,32,625]{3,2,1,0:T(8,128)(2,1)S(1)}, u32[]{:S(2)}, u32[]{:S(2)}) async-start(bf16[16,2,32,625]{3,2,1,0:T(8,128)(2,1)} %bitcast.33), calls=%async_computation.1 | async-start | bytes 2621440 | tf_op jit(solution)/shard_map/all_to_all | solution.py:48
  66.1 15.7 %copy-start.1 = (f32[1,64,64]{2,1,0:T(8,128)S(1)}, f32[1,64,64]{2,1,0:T(8,128)}, u32[]{:S(2)}) copy-start(f32[1,64,64]{2,1,0:T(8,128)} %param.15) | copy-start | bytes 49156
  71.5 1.2 %collective-permute-start = (f32[32,64]{1,0:T(8,128)S(1)}, f32[32,64]{1,0:T(8,128)S(1)}, u32[]{:S(2)}, u32[]{:S(2)}) collective-permute-start(f32[32,64]{1,0:T(8,128)S(1)} %convolution_bitcast_fusion.1), channel_id=1, source_target_pairs={{0,1},{1,0},{2,3},{3,2},{4,5},{5,4},{6,7},{7,6},{8,9},{9,8},{10,11... | collective-permute-start | bytes 24584 | tf_op jit(solution)/shard_map/ppermute | solution.py:77
  72.7 3.7 %collective-permute-start.1 = (f32[32,64]{1,0:T(8,128)S(1)}, f32[32,64]{1,0:T(8,128)S(1)}, u32[]{:S(2)}, u32[]{:S(2)}) collective-permute-start(f32[32,64]{1,0:T(8,128)S(1)} %add.27), channel_id=1, source_target_pairs={{0,2},{1,3},{2,0},{3,1},{4,6},{5,7},{6,4},{7,5},{8,10},{9,11},{10,... | collective-permute-start | bytes 24584 | tf_op jit(solution)/shard_map/ppermute | solution.py:77
  76.5 5.2 %collective-permute-start.2 = (f32[32,64]{1,0:T(8,128)S(1)}, f32[32,64]{1,0:T(8,128)S(1)}, u32[]{:S(2)}, u32[]{:S(2)}) collective-permute-start(f32[32,64]{1,0:T(8,128)S(1)} %add.28), channel_id=1, source_target_pairs={{0,4},{1,5},{2,6},{3,7},{4,0},{5,1},{6,2},{7,3},{8,12},{9,13},{10,... | collective-permute-start | bytes 24584 | tf_op jit(solution)/shard_map/ppermute | solution.py:77
